TPU v7x, 512 devices: a whole 4x4x16 slice. The times are simulated.
512 devices in a mesh: section: 2 (over core), dp: 64 (over z, x), mp: 4 (over y).
Axes of the slice: x: 4, y: 4, z: 16, core: 2. Of those that a mesh axis runs over, the one named last changes fastest.
Arguments:
- states: bfloat16 [512, 24, 4096], P('dp')
- norm_gain: float32 [4096], replicated, may hold values from 0.1 to 1.9
- key_weight: bfloat16 [4096, 4096], P('dp', ('section', 'mp')), may hold values from -0.09375 to 0.09375
- value_weight: bfloat16 [4096, 4096], P('dp', ('section', 'mp')), may hold values from -0.09375 to 0.09375
- pass_len: int32 [512], P('dp'), may hold values from 1 to 24
- retrieval: int32 [64, 64], replicated, may hold values from 0 to 511, as said below
- queries: bfloat16 [64, 32, 4096], P('dp', None, ('section', 'mp'))
Outputs:
- context: bfloat16 [64, 32, 4096], P('dp', None, ('section', 'mp'))
- passage_scores: float32 [64, 64], P('dp')
Inputs may be any that keep to these rules, and one draw needn't show every extreme that they name: `retrieval`: each question's list names 64 different passages. Counting passages of one block of 8 ids (the same id // 8), a list names passages of between 32 and 63 different blocks, at most 2 from any block, and exactly 2 from at least one. Popular passages recur in many lists.
All inputs are finite; a program needn't handle non-finite values.
Results may differ from a plain program's by a relative error of at most 0.013.
Values may be sent and summed in bfloat16 or wider, within the bound.
No kernel may reach another device: no remote copies, remote signals or barrier semaphores. Data moves between devices by JAX's collectives and lax.ppermute only.
A program may use at most 128 MiB of HBM per device.

v0:
```python
import jax
import jax.numpy as jnp
from jax import lax
from jax.sharding import PartitionSpec as P

HS = 64
CAP = 2


def local(states, norm_gain, key_weight, value_weight, pass_len, retrieval, queries):
    blocks, tokens, model_width = states.shape
    inner_width = key_weight.shape[1]
    heads_here = inner_width // HS
    widened = states.astype(jnp.float32)
    mean_square = jnp.mean(widened * widened, axis=-1, keepdims=True)
    normed = (widened * lax.rsqrt(mean_square + 1e-06) * norm_gain).astype(jnp.bfloat16)
    flat_rows = normed.reshape(blocks * tokens, model_width)
    keys_full = jnp.dot(
        flat_rows,
        lax.all_gather(key_weight, "dp", axis=0, tiled=True),
        preferred_element_type=jnp.float32,
    )
    values_full = jnp.dot(
        flat_rows,
        lax.all_gather(value_weight, "dp", axis=0, tiled=True),
        preferred_element_type=jnp.float32,
    )
    keys = keys_full.astype(jnp.bfloat16).reshape(blocks, tokens, inner_width)
    values = values_full.astype(jnp.bfloat16).reshape(blocks, tokens, inner_width)
    owner_index = lax.axis_index("dp")
    owners = lax.axis_size("dp")
    retrieved = retrieval.shape[1]
    owner_of = retrieval // blocks
    is_mine = owner_of == owner_index
    order_rank = jnp.cumsum(is_mine.astype(jnp.int32), axis=1) - 1
    local_ids = retrieval % blocks
    picked_list = []
    valid_list = []
    for slot_index in range(CAP):
        selected = is_mine & (order_rank == slot_index)
        picked_list.append(jnp.sum(jnp.where(selected, local_ids, 0), axis=1))
        valid_list.append(jnp.any(selected, axis=1))
    picked = jnp.stack(picked_list, axis=1)
    is_valid = jnp.stack(valid_list, axis=1)
    send_len = jnp.where(is_valid, pass_len[picked], 0)
    my_list = lax.dynamic_slice_in_dim(retrieval, owner_index, 1, 0)[0]
    list_owner = my_list // blocks
    slot_ids = jnp.arange(retrieved, dtype=jnp.int32)
    earlier_same = (list_owner[:, None] == list_owner[None, :]) & (
        slot_ids[None, :] < slot_ids[:, None]
    )
    list_rank = jnp.sum(earlier_same.astype(jnp.int32), axis=1)
    where_from = list_owner * CAP + list_rank
    query_here = queries[0]
    answer_len = query_here.shape[0]
    positions = jnp.arange(tokens, dtype=jnp.int32)
    send_keys = keys[picked]
    send_values = values[picked]
    got_keys, got_values, got_len = (
        lax.all_to_all(send_keys, "dp", split_axis=0, concat_axis=0, tiled=True),
        lax.all_to_all(send_values, "dp", split_axis=0, concat_axis=0, tiled=True),
        lax.all_to_all(send_len, "dp", split_axis=0, concat_axis=0, tiled=True),
    )
    chosen_keys = got_keys.reshape(owners * CAP, tokens, inner_width)[where_from].reshape(
        retrieved * tokens, heads_here, HS
    )
    chosen_values = got_values.reshape(owners * CAP, tokens, inner_width)[where_from].reshape(
        retrieved * tokens, heads_here, HS
    )
    chosen_len = got_len.reshape(owners * CAP)[where_from]
    is_live = (positions[None, :] < chosen_len[:, None]).reshape(retrieved * tokens)
    query_heads = query_here.reshape(answer_len, heads_here, HS)
    scores = jnp.einsum(
        "thd,lhd->htl", query_heads, chosen_keys, preferred_element_type=jnp.float32
    )
    scores = jnp.where(is_live[None, None, :], scores, -jnp.inf)
    row_max = jnp.max(scores, axis=-1, keepdims=True)
    exponent = jnp.exp(scores - row_max)
    row_total = jnp.sum(exponent, axis=-1, keepdims=True)
    weights = exponent / row_total
    context = jnp.einsum(
        "htl,lhd->thd", weights, chosen_values.astype(jnp.float32), precision=lax.Precision.HIGHEST
    )
    passage_mass = (
        weights.reshape(heads_here, answer_len, retrieved, tokens)
        .sum(axis=-1)
        .sum(axis=0)
        .mean(axis=0)
    )
    passage_scores = lax.psum(passage_mass, ("section", "mp"))
    context_out = context.reshape(answer_len, inner_width).astype(jnp.bfloat16)
    return (context_out[None], passage_scores[None])


def solution(mesh):
    in_specs = (
        P("dp", None, None),
        P(),
        P("dp", ("section", "mp")),
        P("dp", ("section", "mp")),
        P("dp"),
        P(),
        P("dp", None, ("section", "mp")),
    )
    out_specs = (P("dp", None, ("section", "mp")), P("dp", None))
    return jax.shard_map(local, mesh=mesh, in_specs=in_specs, out_specs=out_specs, check_vma=False)
```

profile of v0, /device:TPU:7, one launch (start us, length us, event | category | flops | bytes accessed | tf_op | source)
XLA Modules:
  0.0 516.2 jit_solution(7482054815489007889)
XLA Ops:
  7.2 0.0 copy-start
  7.2 0.0 copy-start.3
  7.2 0.0 all-gather.5.cloned.1.call-start
  7.2 0.7 all-gather.5.cloned.1.call-update
  7.9 0.8 fusion.33
  8.7 0.2 reduce_window_sum.11
  8.9 0.1 fusion.32
  9.1 0.9 select_reduce_fusion.1
  10.0 1.6 fusion.35
  11.6 4.4 compare_select_fusion.1
  16.0 0.7 add_select_fusion.2
  16.6 0.7 copy.25
  17.4 18.0 %all-to-all-start.1 = ((s32[64,1,2]{2,1,0:T(1,128)}), s32[64,1,2]{2,1,0:T(1,128)S(1)}, u32[]{:S(2)}, u32[]{:S(2)}) async-start(s32[64,1,2]{2,1,0:T(1,128)} %copy.25), calls=%async_computation.1 | async-start | bytes 65536 | tf_op jit(solution)/shard_map/all_to_all | solution.py:62
  35.4 0.1 copy.24
  35.5 0.1 reshape.299
  35.6 1.8 fusion
  37.4 0.0 copy-done
  37.5 0.0 copy-done.3
  37.5 0.5 fusion.2
  37.9 0.0 copy-start.1
  37.9 112.6 %all-gather.5.cloned.1.call-done = bf16[4096,512]{1,0:T(8,128)(2,1)} async-done(((bf16[64,512]{1,0:T(8,128)(2,1)}), bf16[4096,512]{1,0:T(8,128)(2,1)}) %all-gather.5.cloned.1.call-update) | async-done | bytes 4194320 | tf_op jit(solution)/shard_map/all_gather | solution.py:20
  150.6 3.2 convolution_convert_fusion
  153.8 0.0 copy-done.1
  153.8 2.4 gather_fusion.3
  156.2 0.0 all-to-all-done.1
  156.2 10.4 %all-to-all-start.2 = ((bf16[64,2,24,512]{3,2,1,0:T(8,128)(2,1)}), bf16[64,2,24,512]{3,2,1,0:T(8,128)(2,1)S(1)}, u32[]{:S(2)}, u32[]{:S(2)}) async-start(bf16[64,2,24,512]{3,2,1,0:T(8,128)(2,1)} %bitcast.24), calls=%async_computation.2 | async-start | bytes 6291456 | tf_op jit(solution)/shard_map/all_to_all | solution.py:60
  166.6 0.0 all-gather.3.cloned.1.call-start
  166.6 0.7 all-gather.3.cloned.1.call-update
  167.3 178.6 %all-gather.3.cloned.1.call-done = bf16[4096,512]{1,0:T(8,128)(2,1)} async-done(((bf16[64,512]{1,0:T(8,128)(2,1)}), bf16[4096,512]{1,0:T(8,128)(2,1)}) %all-gather.3.cloned.1.call-update) | async-done | bytes 4194320 | tf_op jit(solution)/shard_map/all_gather | solution.py:25
  345.9 3.6 convolution_convert_fusion.1
  349.6 2.4 gather_fusion
  352.0 0.0 all-to-all-done.2
  352.0 0.0 copy-start.2
  352.0 10.5 %all-to-all-start = ((bf16[64,2,24,512]{3,2,1,0:T(8,128)(2,1)}), bf16[64,2,24,512]{3,2,1,0:T(8,128)(2,1)}, u32[]{:S(2)}, u32[]{:S(2)}) async-start(bf16[64,2,24,512]{3,2,1,0:T(8,128)(2,1)} %bitcast.4), calls=%async_computation | async-start | bytes 6291456 | tf_op jit(solution)/shard_map/all_to_all | solution.py:61
  362.5 0.0 copy-done.2
  362.5 0.1 reshape_squeeze.3
  362.6 0.7 and_select_fusion.1
  363.3 0.7 fusion.30
  364.0 0.2 convert_reduce_fusion
  364.2 0.7 fusion.29
  364.9 0.5 broadcast.291
  365.5 0.7 reduce.7
  366.2 0.1 reshape.293
  366.3 0.8 gather_fusion.2
  367.1 0.1 iota_compare_fusion
  367.2 0.1 lt.76
  367.3 1.8 gather_fusion.4
  369.1 5.2 %reshape.296 = bf16[1536,8,64]{2,1,0:T(8,128)(2,1)} reshape(bf16[64,24,512]{2,1,0:T(8,128)(2,1)} %gather_fusion.4) | data formatting | bytes 3145728 | tf_op jit(solution)/shard_map/reshape | solution.py:64
  374.3 3.1 fusion.36
  377.4 0.4 fusion.14
  377.7 0.4 fusion.21
  378.1 0.1 reduce_sum.78
  378.2 0.1 reduce_sum.79
  378.3 23.3 %psum.7 = f32[1,64]{1,0:T(1,128)} all-reduce(f32[1,64]{1,0:T(1,128)S(1)} %multiply_bitcast_fusion), channel_id=1, replica_groups=mesh['section'=2,'dp'=64,'mp'=4] {'section','mp'}, use_global_device_ids=true, to_apply=%region_11.12 | all-reduce | flops 64 | bytes 512 | tf_op jit(solution)/shard_map/psum | solution.py:90
  401.7 97.5 %all-to-all-done = bf16[64,2,24,512]{3,2,1,0:T(8,128)(2,1)} async-done(((bf16[64,2,24,512]{3,2,1,0:T(8,128)(2,1)}), bf16[64,2,24,512]{3,2,1,0:T(8,128)(2,1)}, u32[]{:S(2)}, u32[]{:S(2)}) %all-to-all-start) | async-done | bytes 3145760 | tf_op jit(solution)/shard_map/all_to_all | solution.py:61
  499.1 2.5 gather_fusion.1
  501.7 3.0 reshape.292
  504.7 3.9 fusion.18
  508.6 0.7 convert_element_type.43
  (6 shorter events, 0.1 us)
Async XLA Ops:
  7.2 30.3 %copy-start = (bf16[8,24,4096]{2,1,0:T(8,128)(2,1)S(1)}, bf16[8,24,4096]{2,1,0:T(8,128)(2,1)}, u32[]{:S(2)}) copy-start(bf16[8,24,4096]{2,1,0:T(8,128)(2,1)} %param.7) | copy-start | bytes 4718596
  7.2 30.3 %copy-start.3 = (f32[4096]{0:T(1024)S(1)}, f32[4096]{0:T(1024)}, u32[]{:S(2)}) copy-start(f32[4096]{0:T(1024)} %param.8) | copy-start | bytes 49156
  7.2 143.4 %all-gather.5.cloned.1.call-start = ((), (), s32[]{:S(2)}) async-start(), calls=%async_computation.4 | async-start | bytes 4259840 | tf_op jit(solution)/shard_map/all_gather | solution.py:20
  17.4 138.8 %all-to-all-start.1 = ((s32[64,1,2]{2,1,0:T(1,128)}), s32[64,1,2]{2,1,0:T(1,128)S(1)}, u32[]{:S(2)}, u32[]{:S(2)}) async-start(s32[64,1,2]{2,1,0:T(1,128)} %copy.25), calls=%async_computation.1 | async-start | bytes 65536 | tf_op jit(solution)/shard_map/all_to_all | solution.py:62
  37.9 115.8 %copy-start.1 = (bf16[8,24,4096]{2,1,0:T(8,128)(2,1)}, bf16[8,24,4096]{2,1,0:T(8,128)(2,1)S(1)}, u32[]{:S(2)}) copy-start(bf16[8,24,4096]{2,1,0:T(8,128)(2,1)S(1)} %fusion.2) | copy-start | bytes 4718596
  156.2 195.8 %all-to-all-start.2 = ((bf16[64,2,24,512]{3,2,1,0:T(8,128)(2,1)}), bf16[64,2,24,512]{3,2,1,0:T(8,128)(2,1)S(1)}, u32[]{:S(2)}, u32[]{:S(2)}) async-start(bf16[64,2,24,512]{3,2,1,0:T(8,128)(2,1)} %bitcast.24), calls=%async_computation.2 | async-start | bytes 6291456 | tf_op jit(solution)/shard_map/all_to_all | solution.py:60
  166.6 179.3 %all-gather.3.cloned.1.call-start = ((), (), s32[]{:S(2)}) async-start(), calls=%async_computation.3 | async-start | bytes 4259840 | tf_op jit(solution)/shard_map/all_gather | solution.py:25
  352.0 10.5 %copy-start.2 = (bf16[1,32,512]{2,1,0:T(8,128)(2,1)S(1)}, bf16[1,32,512]{2,1,0:T(8,128)(2,1)}, u32[]{:S(2)}) copy-start(bf16[1,32,512]{2,1,0:T(8,128)(2,1)} %param.13) | copy-start | bytes 98308
  352.0 147.2 %all-to-all-start = ((bf16[64,2,24,512]{3,2,1,0:T(8,128)(2,1)}), bf16[64,2,24,512]{3,2,1,0:T(8,128)(2,1)}, u32[]{:S(2)}, u32[]{:S(2)}) async-start(bf16[64,2,24,512]{3,2,1,0:T(8,128)(2,1)} %bitcast.4), calls=%async_computation | async-start | bytes 6291456 | tf_op jit(solution)/shard_map/all_to_all | solution.py:61
Sparse Core Ops, SparseCore 0:
  10.9 139.6 all-gather.4
  170.4 175.5 all-gather.2
where the time goes:
time: 526 us; the launch traced here: 516 us
  waiting for transfers between devices  390 us (74%)
  starting transfers between devices  39 us (7%)
  blocking collectives  23.3 us (4%)
  local copies, waits for them, and re-layouts  22.5 us (4%)
  between operations  14.2 us (3%)
  matrix products  13.8 us (3%)
  other arithmetic  13.3 us (3%)
    all_gather x1, waiting for transfers between devices, local(): lax.all_gather(value_weight, 'dp', axis=0, tiled=True)  179 us
    all_gather x1, waiting for transfers between devices, local(): lax.all_gather(key_weight, 'dp', axis=0, tiled=True)  113 us
    all_to_all x1, waiting for transfers between devices, local(): lax.all_to_all(send_values, 'dp', split_axis=0, concat_axis=0, tiled=True)  97.5 us
    psum x1, blocking collectives, local(): passage_scores = lax.psum(passage_mass, ('section', 'mp'))  23.3 us
    all_to_all x1, starting transfers between devices, local(): lax.all_to_all(send_len, 'dp', split_axis=0, concat_axis=0, tiled=True)  18 us
    all_to_all x1, starting transfers between devices, local(): lax.all_to_all(send_values, 'dp', split_axis=0, concat_axis=0, tiled=True)  10.5 us
  transfers between devices with their start and end apart: 5, of which 3 were waited for; matrix products, arithmetic and copies ran while one was open for 8% of the time, Pallas kernels for 0%

commit v1 on v0

v1 whole, which is shorter than its diff:
```python
import jax
import jax.numpy as jnp
from jax import lax
from jax.sharding import PartitionSpec as P

HS = 64
WIRE = jnp.bfloat16


def _plane_shape(mesh):
    n_dp = mesh.shape["dp"]
    try:
        xs = {d.coords[0] for d in mesh.devices[0, :, 0]}
        nx = len(xs)
    except Exception:
        nx = 2 if n_dp % 2 == 0 else 1
    return n_dp // nx, nx


def _ring_perm(nz, nx, along, step):
    pairs = []
    for z in range(nz):
        for x in range(nx):
            if along == "x":
                dst = z * nx + (x + step) % nx
            else:
                dst = ((z + step) % nz) * nx + x
            pairs.append((z * nx + x, dst))
    return pairs


def _send(tree, perm):
    return jax.tree.map(lambda a: lax.ppermute(a, "dp", perm), tree)


def _gather_ring(block, n, fwd, bwd):
    if n == 1:
        return block[None]
    rel = [None] * n
    rel[0] = block
    f = block
    g = block
    for k in range(1, (n - 1) // 2 + 1):
        f = lax.ppermute(f, "dp", fwd)
        g = lax.ppermute(g, "dp", bwd)
        rel[n - k] = f
        rel[k] = g
    if n % 2 == 0:
        half = n // 2
        if block.shape[0] >= 2:
            cut = block.shape[0] // 2
            a = lax.ppermute(f[:cut], "dp", fwd)
            b = lax.ppermute(g[cut:], "dp", bwd)
            rel[half] = jnp.concatenate([a, b], axis=0)
        else:
            rel[half] = lax.ppermute(f, "dp", fwd)
    return jnp.stack(rel)


def _combine(a, b):
    ma, la, oa, ea = a
    mb, lb, ob, eb = b
    m = jnp.maximum(ma, mb)
    sa = jnp.where(ma == m, 1.0, jnp.exp(ma - m))
    sb = jnp.where(mb == m, 1.0, jnp.exp(mb - m))
    l = sa * la + sb * lb
    sa_o = jnp.swapaxes(sa, -1, -2)[..., None]
    sb_o = jnp.swapaxes(sb, -1, -2)[..., None]
    o = oa * sa_o + ob * sb_o
    e = ea * sa[..., None] + eb * sb[..., None]
    return (m, l, o, e)


def _to_wire(s):
    m, l, o, e = s
    return (m, l, o.astype(WIRE), e.astype(WIRE))


def _from_wire(s):
    m, l, o, e = s
    return (m, l, o.astype(jnp.float32), e.astype(jnp.float32))


def _reduce_ring(state, axis, me, n, fwd, bwd):
    def chunk(r):
        idx = (me + r) % n
        return jax.tree.map(lambda a: lax.dynamic_index_in_dim(a, idx, axis, keepdims=False), state)

    if n == 1:
        return chunk(0)
    nb = n // 2
    nf = n - 1 - nb
    bacc = chunk(n - nb)
    facc = None
    result = None
    for k in range(1, nb + 1):
        if nf > 0 and k == nb - nf + 1:
            facc = chunk(nf)
        recv_b = _from_wire(_send(_to_wire(bacc), bwd))
        recv_f = _from_wire(_send(_to_wire(facc), fwd)) if facc is not None else None
        if k < nb:
            bacc = _combine(recv_b, chunk((k - nb) % n))
            if recv_f is not None:
                facc = _combine(recv_f, chunk(nb - k))
        else:
            result = _combine(chunk(0), recv_b)
            if recv_f is not None:
                result = _combine(result, recv_f)
    return result


def _local(nz, nx, states, norm_gain, key_weight, value_weight, pass_len, retrieval, queries):
    blocks, tokens, model_width = states.shape
    inner = key_weight.shape[1]
    heads = inner // HS
    rows_here = key_weight.shape[0]
    n_dp = nz * nx
    dpi = lax.axis_index("dp")
    zi = dpi // nx
    xi = dpi % nx
    xf = _ring_perm(nz, nx, "x", 1)
    xb = _ring_perm(nz, nx, "x", -1)
    zf = _ring_perm(nz, nx, "z", 1)
    zb = _ring_perm(nz, nx, "z", -1)

    wkv = jnp.concatenate([key_weight, value_weight], axis=1)
    wx = _gather_ring(wkv, nx, xf, xb)
    wzx = _gather_ring(wx, nz, zf, zb)

    q_all = lax.all_gather(queries, "dp", axis=0, tiled=True)

    widened = states.astype(jnp.float32)
    mean_square = jnp.mean(widened * widened, axis=-1, keepdims=True)
    normed = (widened * lax.rsqrt(mean_square + 1e-06) * norm_gain).astype(jnp.bfloat16)
    flat = normed.reshape(blocks * tokens, nz, nx, rows_here)
    flat = jnp.roll(flat, -zi, axis=1)
    flat = jnp.roll(flat, -xi, axis=2)
    kv = jnp.dot(
        flat.reshape(blocks * tokens, model_width),
        wzx.reshape(model_width, 2 * inner),
        preferred_element_type=jnp.float32,
    ).astype(jnp.bfloat16)
    keys = kv[:, :inner].reshape(blocks, tokens, heads, HS)
    values = kv[:, inner:].reshape(blocks, tokens, heads, HS)

    n_q, answer_len, _ = q_all.shape
    q_heads = q_all.reshape(n_q, answer_len, heads, HS)
    scores = jnp.einsum("qthe,pshe->qhtps", q_heads, keys, preferred_element_type=jnp.float32)
    local_ids = retrieval - dpi * blocks
    owned = (local_ids >= 0) & (local_ids < blocks)
    onehot = (local_ids[:, None, :] == jnp.arange(blocks, dtype=jnp.int32)[None, :, None]) & owned[:, None, :]
    picked = jnp.any(onehot, axis=2)
    positions = jnp.arange(tokens, dtype=jnp.int32)
    live = picked[:, :, None] & (positions[None, None, :] < pass_len[None, :, None])
    live5 = live[:, None, None, :, :]
    masked = jnp.where(live5, scores, -jnp.inf)
    m_loc = jnp.max(masked, axis=(3, 4))
    e = jnp.where(live5, jnp.exp(scores - m_loc[..., None, None]), 0.0)
    l_loc = jnp.sum(e, axis=(3, 4))
    e_pass = jnp.sum(e, axis=4)
    e_slot = jnp.einsum(
        "qhtp,qpj->qhtj", e_pass, onehot.astype(jnp.float32), precision=lax.Precision.HIGHEST
    )
    o_loc = jnp.einsum(
        "qhtps,pshe->qthe", e, values.astype(jnp.float32), precision=lax.Precision.HIGHEST
    )

    n_local_q = n_q // n_dp
    def split_q(a):
        return a.reshape((nz, nx, n_local_q) + a.shape[1:])
    state = jax.tree.map(split_q, (m_loc, l_loc, o_loc, e_slot))
    state = _reduce_ring(state, 1, xi, nx, xf, xb)
    state = _reduce_ring(state, 0, zi, nz, zf, zb)
    m_fin, l_fin, o_fin, e_fin = state
    context = o_fin / jnp.swapaxes(l_fin, -1, -2)[..., None]
    context = context.reshape(n_local_q, answer_len, inner).astype(jnp.bfloat16)
    mass = jnp.sum(e_fin / l_fin[..., None], axis=(1, 2)) / answer_len
    mass = lax.psum(mass, ("section", "mp"))
    return (context, mass)


def solution(mesh):
    nz, nx = _plane_shape(mesh)
    in_specs = (
        P("dp", None, None),
        P(),
        P("dp", ("section", "mp")),
        P("dp", ("section", "mp")),
        P("dp"),
        P(),
        P("dp", None, ("section", "mp")),
    )
    out_specs = (P("dp", None, ("section", "mp")), P("dp", None))

    def body(*args):
        return _local(nz, nx, *args)

    return jax.shard_map(body, mesh=mesh, in_specs=in_specs, out_specs=out_specs, check_vma=False)
```

time: 526 us -> 690 us (1.31)
  the two profiles are of different devices: /device:TPU:7 before, /device:TPU:1 now
where the time goes in v1:
time: 690 us; the launch traced here: 678 us
  starting transfers between devices  303 us (44%)
  waiting for transfers between devices  96.9 us (14%)
  local copies, waits for them, and re-layouts  91.3 us (13%)
  other arithmetic  70.6 us (10%)
  blocking collectives  51 us (7%)
  matrix products  46.9 us (7%)
  between operations  17.8 us (3%)
    ppermute x72, starting transfers between devices, _send(): return jax.tree.map(lambda a: lax.ppermute(a, 'dp', perm), tree)  228 us
    psum x1, blocking collectives, _local(): mass = lax.psum(mass, ('section', 'mp'))  51 us
    all_gather x1, waiting for transfers between devices, _local(): q_all = lax.all_gather(queries, 'dp', axis=0, tiled=True)  46.2 us
    ppermute x8, starting transfers between devices, _gather_ring(): g = lax.ppermute(g, 'dp', bwd)  45.1 us
    mul x36, local copies, waits for them, and re-layouts, _combine(): o = oa * sa_o + ob * sb_o  43.7 us
    ppermute x8, waiting for transfers between devices, _gather_ring(): g = lax.ppermute(g, 'dp', bwd)  23 us
    reduce_sum x1, other arithmetic, _local(): e_pass = jnp.sum(e, axis=4)  22.8 us
    dot_general x1, matrix products, _local(): jnp.einsum('qthe,pshe->qhtps', q_heads, keys, preferred_element_type=jnp....  20 us
  transfers between devices with their start and end apart: 93, of which 20 were waited for; matrix products, arithmetic and copies ran while one was open for 22% of the time, Pallas kernels for 0%

profile of v1, /device:TPU:1, one launch (start us, length us, event | category | flops | bytes accessed | tf_op | source)
XLA Modules:
  0.0 677.8 jit_solution(13137495287411351185)
XLA Ops:
  9.0 3.9 collective-permute-start.1
  18.7 4.4 collective-permute-start.3
  25.1 11.3 %collective-permute-start.4 = (bf16[4,64,1024]{2,1,0:T(8,128)(2,1)S(1)}, bf16[4,64,1024]{2,1,0:T(8,128)(2,1)S(1)}, u32[]{:S(2)}, u32[]{:S(2)}) collective-permute-start(bf16[4,64,1024]{2,1,0:T(8,128)(2,1)S(1)} %pad_maximum_fusion), channel_id=1, source_target_pairs={{0,240},{4,244},{8,248},{12,252},{16,0},{20,4},{24,8},{28,12},{32,... | collective-permute-start | bytes 1572872 | tf_op jit(solution)/shard_map/ppermute | solution.py:45
  38.3 6.7 collective-permute-done.4
  45.0 5.3 collective-permute-start.5
  52.3 5.8 collective-permute-done.5
  58.0 5.4 collective-permute-start.6
  67.3 3.4 collective-permute-done.6
  70.7 5.3 collective-permute-start.7
  79.6 4.3 reshape.801
  83.9 4.7 copy.71
  91.3 4.6 collective-permute-start.8
  99.3 3.4 collective-permute-done.8
  102.7 5.1 collective-permute-start.9
  111.1 3.7 collective-permute-done.9
  114.8 4.9 collective-permute-start.10
  125.3 8.0 %collective-permute-done.17 = bf16[4,64,1024]{2,1,0:T(8,128)(2,1)S(1)} collective-permute-done((bf16[4,64,1024]{2,1,0:T(8,128)(2,1)S(1)}, bf16[4,64,1024]{2,1,0:T(8,128)(2,1)S(1)}, u32[]{:S(2)}, u32[]{:S(2)}) %collective-permute-start.17) | collective-permute-done | bytes 524320 | tf_op jit(solution)/shard_map/ppermute | solution.py:44
  135.3 4.6 collective-permute-start.19
  139.9 4.8 collective-permute-done.18
  151.7 46.2 %all-gather.2.cloned.1.call-done = bf16[64,32,512]{2,1,0:T(8,128)(2,1)} async-done(((bf16[1,32,512]{2,1,0:T(8,128)(2,1)}), bf16[64,32,512]{2,1,0:T(8,128)(2,1)}) %all-gather.2.cloned.1.call-update) | async-done | bytes 2097168 | tf_op jit(solution)/shard_map/all_gather | solution.py:130
  197.8 6.7 reshape.804
  204.5 20.0 %fusion = (f32[64,8,32]{0,2,1:T(8,128)S(1)}, f32[8,8,24,64,32]{3,2,4,1,0:T(8,128)}) fusion(pred[64,8,24]{0,2,1:T(8,128)(4,1)S(1)} %broadcast_and_fusion, bf16[64,32,8,64,1]{3,2,1,0,4:T(8,128)(2,1)} %bitcast.753, bf16[8,24,8,64,1]{3,2,1,0,4:T(8,128)(2,1)S(1)} %bitcast.760), kind=kOutput, calls=%fused_computation.2 | convolution fusion | flops 408928256 | bytes 14954496 | tf_op jit(solution)/shard_map/qthe,pshe->qhtps/dot_general | solution.py:148
  224.7 22.8 %fusion.243 = (f32[64,8,32,8]{0,2,3,1:T(8,128)S(1)}, f32[64,8,32]{0,2,1:T(8,128)S(1)}, f32[64,8,32,8,24]{0,4,2,3,1:T(8,128)}) fusion(f32[64,8,32]{0,2,1:T(8,128)S(1)} %get-tuple-element.164, f32[8,8,24,64,32]{3,2,4,1,0:T(8,128)} %get-tuple-element.165, pred[64,8,24]{0,2,1:T(8,128)(4,1)S(1)} %broadcast_and_fusion), kind=kLoop, calls=%fused_computation.390 | loop fusion | flops 12435456 | bytes 25833472 | tf_op jit(solution)/shard_map/reduce_sum | solution.py:160
  247.5 3.5 collective-permute-start.20
  264.9 4.0 collective-permute-start.26
  270.2 4.8 collective-permute-start.27
  276.4 5.0 collective-permute-start.28
  282.8 4.8 collective-permute-start.29
  290.2 4.6 collective-permute-start.30
  296.1 4.8 collective-permute-start.31
  302.9 3.6 collective-permute-done.43
  309.0 3.5 collective-permute-start.44
  316.5 4.6 collective-permute-start.57
  329.4 4.3 collective-permute-start.59
  333.7 7.5 %fusion.43 = f32[64,8,32,64]{3,2,1,0:T(8,128)S(1)} fusion(f32[64,8,32,8]{2,3,1,0:T(8,128)S(1)} %copy.118, s32[64,64]{1,0:T(8,128)} %copy-done.22, pred[64,64]{1,0:T(8,128)(4,1)S(1)} %get-tuple-element.71), kind=kOutput, calls=%fused_computation.70 | convolution fusion | flops 100728832 | bytes 4739072 | tf_op jit(solution)/shard_map/qhtp,qpj->qhtj/dot_general | solution.py:161
  344.6 4.1 collective-permute-start.60
  352.2 3.4 collective-permute-start.76
  359.1 3.6 collective-permute-start.68
  362.7 16.9 %fusion.7 = f32[64,32,8,64]{0,3,1,2:T(8,128)} fusion(f32[64,8,32,8,24]{0,4,2,3,1:T(8,128)} %get-tuple-element.70, bf16[8,24,8,64,1]{3,2,1,0,4:T(8,128)(2,1)S(1)} %bitcast.759), kind=kOutput, calls=%fused_computation.15 | convolution fusion | flops 2415919104 | bytes 16973824 | tf_op jit(solution)/shard_map/qhtps,pshe->qthe/dot_general | solution.py:164
  379.6 9.8 %copy.78 = f32[64,32,8,64]{3,2,1,0:T(8,128)} copy(f32[64,32,8,64]{0,3,1,2:T(8,128)} %fusion.7) | data formatting | bytes 8388608 | tf_op jit(solution)/shard_map/qhtps,pshe->qthe/transpose | solution.py:164
  396.1 3.6 fusion.33
  412.8 4.5 collective-permute-start.63
  431.3 4.6 collective-permute-start.64
  449.8 4.6 collective-permute-start.65
  467.7 4.6 collective-permute-start.66
  484.7 4.3 collective-permute-start.75
  501.8 4.3 fusion.21
  508.5 4.5 collective-permute-start.77
  515.7 4.2 fusion.26
  520.1 4.7 collective-permute-start.34
  526.9 4.6 collective-permute-start.78
  534.6 4.0 collective-permute-start.79
  541.0 4.6 collective-permute-start.36
  548.4 4.6 collective-permute-start.80
  555.2 4.6 collective-permute-start.37
  562.7 4.6 collective-permute-start.81
  569.5 4.6 collective-permute-start.38
  577.2 4.6 collective-permute-start.82
  583.9 4.6 collective-permute-start.39
  591.4 4.6 collective-permute-start.83
  598.2 4.6 collective-permute-start.40
  604.9 4.6 collective-permute-start.84
  611.7 4.6 collective-permute-start.41
  618.6 51.0 %psum.7 = f32[1,64]{1,0:T(1,128)} all-reduce(f32[1,64]{1,0:T(1,128)S(1)} %multiply_bitcast_fusion), channel_id=1, replica_groups=mesh['section'=2,'dp'=64,'mp'=4] {'section','mp'}, use_global_device_ids=true, to_apply=%region_6.7 | all-reduce | flops 64 | bytes 512 | tf_op jit(solution)/shard_map/psum | solution.py:178
  (489 shorter events, 218.1 us)
Async XLA Ops:
  7.2 190.7 %all-gather.2.cloned.1.call-start = ((), (), s32[]{:S(2)}) async-start(), calls=%async_computation | async-start | bytes 2129920 | tf_op jit(solution)/shard_map/all_gather | solution.py:130
  25.1 19.9 %collective-permute-start.4 = (bf16[4,64,1024]{2,1,0:T(8,128)(2,1)S(1)}, bf16[4,64,1024]{2,1,0:T(8,128)(2,1)S(1)}, u32[]{:S(2)}, u32[]{:S(2)}) collective-permute-start(bf16[4,64,1024]{2,1,0:T(8,128)(2,1)S(1)} %pad_maximum_fusion), channel_id=1, source_target_pairs={{0,240},{4,244},{8,248},{12,252},{16,0},{20,4},{24,8},{28,12},{32,... | collective-permute-start | bytes 1572872 | tf_op jit(solution)/shard_map/ppermute | solution.py:45
  36.4 13.9 %collective-permute-start.11 = (bf16[4,64,1024]{2,1,0:T(8,128)(2,1)S(1)}, bf16[4,64,1024]{2,1,0:T(8,128)(2,1)S(1)}, u32[]{:S(2)}, u32[]{:S(2)}) collective-permute-start(bf16[4,64,1024]{2,1,0:T(8,128)(2,1)S(1)} %pad_maximum_fusion), channel_id=1, source_target_pairs={{0,16},{4,20},{8,24},{12,28},{16,32},{20,36},{24,40},{28,44},{32,4... | collective-permute-start | bytes 1572872 | tf_op jit(solution)/shard_map/ppermute | solution.py:44
  45.0 13.1 %collective-permute-start.5 = (bf16[4,64,1024]{2,1,0:T(8,128)(2,1)S(1)}, bf16[4,64,1024]{2,1,0:T(8,128)(2,1)}, u32[]{:S(2)}, u32[]{:S(2)}) collective-permute-start(bf16[4,64,1024]{2,1,0:T(8,128)(2,1)S(1)} %collective-permute-done.4), channel_id=1, source_target_pairs={{0,240},{4,244},{8,248},{12,252},{16,0},{20,4},{24,8},{28,12},{32,... | collective-permute-start | bytes 1572872 | tf_op jit(solution)/shard_map/ppermute | solution.py:45
  50.3 13.1 %collective-permute-start.12 = (bf16[4,64,1024]{2,1,0:T(8,128)(2,1)S(1)}, bf16[4,64,1024]{2,1,0:T(8,128)(2,1)S(1)}, u32[]{:S(2)}, u32[]{:S(2)}) collective-permute-start(bf16[4,64,1024]{2,1,0:T(8,128)(2,1)S(1)} %collective-permute-done.11), channel_id=1, source_target_pairs={{0,16},{4,20},{8,24},{12,28},{16,32},{20,36},{24,40},{28,44},{32,4... | collective-permute-start | bytes 1572872 | tf_op jit(solution)/shard_map/ppermute | solution.py:44
  58.0 12.6 %collective-permute-start.6 = (bf16[4,64,1024]{2,1,0:T(8,128)(2,1)}, bf16[4,64,1024]{2,1,0:T(8,128)(2,1)}, u32[]{:S(2)}, u32[]{:S(2)}) collective-permute-start(bf16[4,64,1024]{2,1,0:T(8,128)(2,1)} %collective-permute-done.5), channel_id=1, source_target_pairs={{0,240},{4,244},{8,248},{12,252},{16,0},{20,4},{24,8},{28,12},{32,... | collective-permute-start | bytes 1572872 | tf_op jit(solution)/shard_map/ppermute | solution.py:45
  63.5 12.5 %collective-permute-start.13 = (bf16[4,64,1024]{2,1,0:T(8,128)(2,1)S(1)}, bf16[4,64,1024]{2,1,0:T(8,128)(2,1)}, u32[]{:S(2)}, u32[]{:S(2)}) collective-permute-start(bf16[4,64,1024]{2,1,0:T(8,128)(2,1)S(1)} %collective-permute-done.12), channel_id=1, source_target_pairs={{0,16},{4,20},{8,24},{12,28},{16,32},{20,36},{24,40},{28,44},{32,4... | collective-permute-start | bytes 1572872 | tf_op jit(solution)/shard_map/ppermute | solution.py:44
  70.7 20.6 %collective-permute-start.7 = (bf16[4,64,1024]{2,1,0:T(8,128)(2,1)}, bf16[4,64,1024]{2,1,0:T(8,128)(2,1)}, u32[]{:S(2)}, u32[]{:S(2)}) collective-permute-start(bf16[4,64,1024]{2,1,0:T(8,128)(2,1)} %collective-permute-done.6), channel_id=1, source_target_pairs={{0,240},{4,244},{8,248},{12,252},{16,0},{20,4},{24,8},{28,12},{32,... | collective-permute-start | bytes 1572872 | tf_op jit(solution)/shard_map/ppermute | solution.py:45
  76.0 19.9 %collective-permute-start.14 = (bf16[4,64,1024]{2,1,0:T(8,128)(2,1)}, bf16[4,64,1024]{2,1,0:T(8,128)(2,1)}, u32[]{:S(2)}, u32[]{:S(2)}) collective-permute-start(bf16[4,64,1024]{2,1,0:T(8,128)(2,1)} %collective-permute-done.13), channel_id=1, source_target_pairs={{0,16},{4,20},{8,24},{12,28},{16,32},{20,36},{24,40},{28,44},{32,4... | collective-permute-start | bytes 1572872 | tf_op jit(solution)/shard_map/ppermute | solution.py:44
  91.3 11.4 %collective-permute-start.8 = (bf16[4,64,1024]{2,1,0:T(8,128)(2,1)}, bf16[4,64,1024]{2,1,0:T(8,128)(2,1)}, u32[]{:S(2)}, u32[]{:S(2)}) collective-permute-start(bf16[4,64,1024]{2,1,0:T(8,128)(2,1)} %collective-permute-done.7), channel_id=1, source_target_pairs={{0,240},{4,244},{8,248},{12,252},{16,0},{20,4},{24,8},{28,12},{32,... | collective-permute-start | bytes 1572872 | tf_op jit(solution)/shard_map/ppermute | solution.py:45
  95.9 12.1 %collective-permute-start.15 = (bf16[4,64,1024]{2,1,0:T(8,128)(2,1)}, bf16[4,64,1024]{2,1,0:T(8,128)(2,1)}, u32[]{:S(2)}, u32[]{:S(2)}) collective-permute-start(bf16[4,64,1024]{2,1,0:T(8,128)(2,1)} %collective-permute-done.14), channel_id=1, source_target_pairs={{0,16},{4,20},{8,24},{12,28},{16,32},{20,36},{24,40},{28,44},{32,4... | collective-permute-start | bytes 1572872 | tf_op jit(solution)/shard_map/ppermute | solution.py:44
  102.7 12.2 %collective-permute-start.9 = (bf16[4,64,1024]{2,1,0:T(8,128)(2,1)}, bf16[4,64,1024]{2,1,0:T(8,128)(2,1)S(1)}, u32[]{:S(2)}, u32[]{:S(2)}) collective-permute-start(bf16[4,64,1024]{2,1,0:T(8,128)(2,1)} %collective-permute-done.8), channel_id=1, source_target_pairs={{0,240},{4,244},{8,248},{12,252},{16,0},{20,4},{24,8},{28,12},{32,... | collective-permute-start | bytes 1572872 | tf_op jit(solution)/shard_map/ppermute | solution.py:45
  108.0 12.1 %collective-permute-start.16 = (bf16[4,64,1024]{2,1,0:T(8,128)(2,1)}, bf16[4,64,1024]{2,1,0:T(8,128)(2,1)S(1)}, u32[]{:S(2)}, u32[]{:S(2)}) collective-permute-start(bf16[4,64,1024]{2,1,0:T(8,128)(2,1)} %collective-permute-done.15), channel_id=1, source_target_pairs={{0,16},{4,20},{8,24},{12,28},{16,32},{20,36},{24,40},{28,44},{32,4... | collective-permute-start | bytes 1572872 | tf_op jit(solution)/shard_map/ppermute | solution.py:44
  114.8 20.4 %collective-permute-start.10 = (bf16[4,64,1024]{2,1,0:T(8,128)(2,1)S(1)}, bf16[4,64,1024]{2,1,0:T(8,128)(2,1)S(1)}, u32[]{:S(2)}, u32[]{:S(2)}) collective-permute-start(bf16[4,64,1024]{2,1,0:T(8,128)(2,1)S(1)} %collective-permute-done.9), channel_id=1, source_target_pairs={{0,240},{4,244},{8,248},{12,252},{16,0},{20,4},{24,8},{28,12},{32,... | collective-permute-start | bytes 1572872 | tf_op jit(solution)/shard_map/ppermute | solution.py:45
  120.1 13.2 %collective-permute-start.17 = (bf16[4,64,1024]{2,1,0:T(8,128)(2,1)S(1)}, bf16[4,64,1024]{2,1,0:T(8,128)(2,1)S(1)}, u32[]{:S(2)}, u32[]{:S(2)}) collective-permute-start(bf16[4,64,1024]{2,1,0:T(8,128)(2,1)S(1)} %collective-permute-done.16), channel_id=1, source_target_pairs={{0,16},{4,20},{8,24},{12,28},{16,32},{20,36},{24,40},{28,44},{32,4... | collective-permute-start | bytes 1572872 | tf_op jit(solution)/shard_map/ppermute | solution.py:44
  133.3 11.4 %collective-permute-start.18 = (bf16[2,64,1024]{2,1,0:T(8,128)(2,1)S(1)}, bf16[2,64,1024]{2,1,0:T(8,128)(2,1)S(1)}, u32[]{:S(2)}, u32[]{:S(2)}) collective-permute-start(bf16[2,64,1024]{2,1,0:T(8,128)(2,1)S(1)} %slice.26), channel_id=1, source_target_pairs={{0,16},{4,20},{8,24},{12,28},{16,32},{20,36},{24,40},{28,44},{32,4... | collective-permute-start | bytes 786440 | tf_op jit(solution)/shard_map/ppermute | solution.py:52
  307.1 13.9 %collective-permute-start.32 = (f32[1,8,32]{2,1,0:T(8,128)}, f32[1,8,32]{2,1,0:T(8,128)S(1)}, u32[]{:S(2)}, u32[]{:S(2)}) collective-permute-start(f32[1,8,32]{2,1,0:T(8,128)} %get-tuple-element.9), channel_id=1, source_target_pairs={{0,240},{4,244},{8,248},{12,252},{16,0},{20,4},{24,8},{28,12},{32,... | collective-permute-start | bytes 3080 | tf_op jit(solution)/shard_map/ppermute | solution.py:33
  309.0 12.0 %collective-permute-start.44 = (f32[1,8,32]{2,1,0:T(8,128)}, f32[1,8,32]{2,1,0:T(8,128)}, u32[]{:S(2)}, u32[]{:S(2)}) collective-permute-start(f32[1,8,32]{2,1,0:T(8,128)} %get-tuple-element.137), channel_id=1, source_target_pairs={{0,16},{4,20},{8,24},{12,28},{16,32},{20,36},{24,40},{28,44},{32,4... | collective-permute-start | bytes 3080 | tf_op jit(solution)/shard_map/ppermute | solution.py:33
  314.6 13.1 %collective-permute-start.58 = (f32[16,1,8,32]{3,2,0,1:T(8,128)}, f32[16,1,8,32]{3,2,0,1:T(8,128)S(1)}, u32[]{:S(2)}, u32[]{:S(2)}) collective-permute-start(f32[16,1,8,32]{3,2,0,1:T(8,128)} %get-tuple-element.105), channel_id=1, source_target_pairs={{0,4},{4,8},{8,12},{12,0},{16,20},{20,24},{24,28},{28,16},{32,36},... | collective-permute-start | bytes 49160 | tf_op jit(solution)/shard_map/ppermute | solution.py:33
  316.5 11.2 %collective-permute-start.57 = (f32[16,1,8,32]{3,2,0,1:T(8,128)}, f32[16,1,8,32]{3,2,0,1:T(8,128)S(1)}, u32[]{:S(2)}, u32[]{:S(2)}) collective-permute-start(f32[16,1,8,32]{3,2,0,1:T(8,128)} %get-tuple-element.107), channel_id=1, source_target_pairs={{0,12},{4,0},{8,4},{12,8},{16,28},{20,16},{24,20},{28,24},{32,44},... | collective-permute-start | bytes 49160 | tf_op jit(solution)/shard_map/ppermute | solution.py:33
  322.4 21.0 %collective-permute-start.33 = (f32[1,8,32]{2,1,0:T(8,128)S(1)}, f32[1,8,32]{2,1,0:T(8,128)S(1)}, u32[]{:S(2)}, u32[]{:S(2)}) collective-permute-start(f32[1,8,32]{2,1,0:T(8,128)S(1)} %get-tuple-element.7), channel_id=1, source_target_pairs={{0,240},{4,244},{8,248},{12,252},{16,0},{20,4},{24,8},{28,12},{32,... | collective-permute-start | bytes 3080 | tf_op jit(solution)/shard_map/ppermute | solution.py:33
  325.5 17.9 %collective-permute-start.45 = (f32[1,8,32]{2,1,0:T(8,128)S(1)}, f32[1,8,32]{2,1,0:T(8,128)S(1)}, u32[]{:S(2)}, u32[]{:S(2)}) collective-permute-start(f32[1,8,32]{2,1,0:T(8,128)S(1)} %get-tuple-element.133), channel_id=1, source_target_pairs={{0,16},{4,20},{8,24},{12,28},{16,32},{20,36},{24,40},{28,44},{32,4... | collective-permute-start | bytes 3080 | tf_op jit(solution)/shard_map/ppermute | solution.py:33
  329.4 14.1 %collective-permute-start.59 = (f32[1,8,32]{2,1,0:T(8,128)S(1)}, f32[1,8,32]{2,1,0:T(8,128)S(1)}, u32[]{:S(2)}, u32[]{:S(2)}) collective-permute-start(f32[1,8,32]{2,1,0:T(8,128)S(1)} %get-tuple-element.144), channel_id=1, source_target_pairs={{0,240},{4,244},{8,248},{12,252},{16,0},{20,4},{24,8},{28,12},{32,... | collective-permute-start | bytes 3080 | tf_op jit(solution)/shard_map/ppermute | solution.py:33
  341.3 14.5 %collective-permute-start.67 = (f32[1,8,32]{2,1,0:T(8,128)S(1)}, f32[1,8,32]{2,1,0:T(8,128)S(1)}, u32[]{:S(2)}, u32[]{:S(2)}) collective-permute-start(f32[1,8,32]{2,1,0:T(8,128)S(1)} %get-tuple-element.145), channel_id=1, source_target_pairs={{0,16},{4,20},{8,24},{12,28},{16,32},{20,36},{24,40},{28,44},{32,4... | collective-permute-start | bytes 3080 | tf_op jit(solution)/shard_map/ppermute | solution.py:33
  344.6 11.3 %collective-permute-start.60 = (f32[1,8,32]{2,1,0:T(8,128)S(1)}, f32[1,8,32]{2,1,0:T(8,128)S(1)}, u32[]{:S(2)}, u32[]{:S(2)}) collective-permute-start(f32[1,8,32]{2,1,0:T(8,128)S(1)} %get-tuple-element.128), channel_id=1, source_target_pairs={{0,240},{4,244},{8,248},{12,252},{16,0},{20,4},{24,8},{28,12},{32,... | collective-permute-start | bytes 3080 | tf_op jit(solution)/shard_map/ppermute | solution.py:33
  350.3 126.9 %collective-permute-start.74 = (bf16[16,1,8,32,64]{4,3,2,0,1:T(8,128)(2,1)}, bf16[16,1,8,32,64]{4,3,2,0,1:T(8,128)(2,1)S(1)}, u32[]{:S(2)}, u32[]{:S(2)}) collective-permute-start(bf16[16,1,8,32,64]{4,3,2,0,1:T(8,128)(2,1)} %get-tuple-element.73), channel_id=1, source_target_pairs={{0,12},{4,0},{8,4},{12,8},{16,28},{20,16},{24,20},{28,24},{32,44},... | collective-permute-start | bytes 1572872 | tf_op jit(solution)/shard_map/ppermute | solution.py:33
  352.2 149.5 %collective-permute-start.76 = (bf16[16,1,8,32,64]{4,3,2,0,1:T(8,128)(2,1)S(1)}, bf16[16,1,8,32,64]{4,3,2,0,1:T(8,128)(2,1)}, u32[]{:S(2)}, u32[]{:S(2)}) collective-permute-start(bf16[16,1,8,32,64]{4,3,2,0,1:T(8,128)(2,1)S(1)} %get-tuple-element.74), channel_id=1, source_target_pairs={{0,4},{4,8},{8,12},{12,0},{16,20},{20,24},{24,28},{28,16},{32,36},... | collective-permute-start | bytes 1572872 | tf_op jit(solution)/shard_map/ppermute | solution.py:33
  357.2 32.2 %collective-permute-start.61 = (f32[1,8,32]{2,1,0:T(8,128)S(1)}, f32[1,8,32]{2,1,0:T(8,128)S(1)}, u32[]{:S(2)}, u32[]{:S(2)}) collective-permute-start(f32[1,8,32]{2,1,0:T(8,128)S(1)} %get-tuple-element.50), channel_id=1, source_target_pairs={{0,240},{4,244},{8,248},{12,252},{16,0},{20,4},{24,8},{28,12},{32,... | collective-permute-start | bytes 3080 | tf_op jit(solution)/shard_map/ppermute | solution.py:33
  359.1 30.3 %collective-permute-start.68 = (f32[1,8,32]{2,1,0:T(8,128)S(1)}, f32[1,8,32]{2,1,0:T(8,128)S(1)}, u32[]{:S(2)}, u32[]{:S(2)}) collective-permute-start(f32[1,8,32]{2,1,0:T(8,128)S(1)} %get-tuple-element.126), channel_id=1, source_target_pairs={{0,16},{4,20},{8,24},{12,28},{16,32},{20,36},{24,40},{28,44},{32,4... | collective-permute-start | bytes 3080 | tf_op jit(solution)/shard_map/ppermute | solution.py:33
  390.8 20.0 %collective-permute-start.62 = (f32[1,8,32]{2,1,0:T(8,128)}, f32[1,8,32]{2,1,0:T(8,128)S(1)}, u32[]{:S(2)}, u32[]{:S(2)}) collective-permute-start(f32[1,8,32]{2,1,0:T(8,128)} %get-tuple-element.48), channel_id=1, source_target_pairs={{0,240},{4,244},{8,248},{12,252},{16,0},{20,4},{24,8},{28,12},{32,... | collective-permute-start | bytes 3080 | tf_op jit(solution)/shard_map/ppermute | solution.py:33
  393.9 17.5 %collective-permute-start.69 = (f32[1,8,32]{2,1,0:T(8,128)}, f32[1,8,32]{2,1,0:T(8,128)}, u32[]{:S(2)}, u32[]{:S(2)}) collective-permute-start(f32[1,8,32]{2,1,0:T(8,128)} %get-tuple-element.124), channel_id=1, source_target_pairs={{0,16},{4,20},{8,24},{12,28},{16,32},{20,36},{24,40},{28,44},{32,4... | collective-permute-start | bytes 3080 | tf_op jit(solution)/shard_map/ppermute | solution.py:33
  408.2 19.8 %collective-permute-start.46 = (f32[1,8,32]{2,1,0:T(8,128)}, f32[1,8,32]{2,1,0:T(8,128)}, u32[]{:S(2)}, u32[]{:S(2)}) collective-permute-start(f32[1,8,32]{2,1,0:T(8,128)} %get-tuple-element.131), channel_id=1, source_target_pairs={{0,16},{4,20},{8,24},{12,28},{16,32},{20,36},{24,40},{28,44},{32,4... | collective-permute-start | bytes 3080 | tf_op jit(solution)/shard_map/ppermute | solution.py:33
  412.8 15.3 %collective-permute-start.63 = (f32[1,8,32]{2,1,0:T(8,128)}, f32[1,8,32]{2,1,0:T(8,128)}, u32[]{:S(2)}, u32[]{:S(2)}) collective-permute-start(f32[1,8,32]{2,1,0:T(8,128)} %get-tuple-element.46), channel_id=1, source_target_pairs={{0,240},{4,244},{8,248},{12,252},{16,0},{20,4},{24,8},{28,12},{32,... | collective-permute-start | bytes 3080 | tf_op jit(solution)/shard_map/ppermute | solution.py:33
  417.3 10.7 %collective-permute-start.70 = (f32[1,8,32]{2,1,0:T(8,128)}, f32[1,8,32]{2,1,0:T(8,128)}, u32[]{:S(2)}, u32[]{:S(2)}) collective-permute-start(f32[1,8,32]{2,1,0:T(8,128)} %get-tuple-element.122), channel_id=1, source_target_pairs={{0,16},{4,20},{8,24},{12,28},{16,32},{20,36},{24,40},{28,44},{32,4... | collective-permute-start | bytes 3080 | tf_op jit(solution)/shard_map/ppermute | solution.py:33
  429.4 15.9 %collective-permute-start.47 = (f32[1,8,32]{2,1,0:T(8,128)}, f32[1,8,32]{2,1,0:T(8,128)S(1)}, u32[]{:S(2)}, u32[]{:S(2)}) collective-permute-start(f32[1,8,32]{2,1,0:T(8,128)} %get-tuple-element.139), channel_id=1, source_target_pairs={{0,16},{4,20},{8,24},{12,28},{16,32},{20,36},{24,40},{28,44},{32,4... | collective-permute-start | bytes 3080 | tf_op jit(solution)/shard_map/ppermute | solution.py:33
  431.3 17.1 %collective-permute-start.64 = (f32[1,8,32]{2,1,0:T(8,128)}, f32[1,8,32]{2,1,0:T(8,128)}, u32[]{:S(2)}, u32[]{:S(2)}) collective-permute-start(f32[1,8,32]{2,1,0:T(8,128)} %get-tuple-element.44), channel_id=1, source_target_pairs={{0,240},{4,244},{8,248},{12,252},{16,0},{20,4},{24,8},{28,12},{32,... | collective-permute-start | bytes 3080 | tf_op jit(solution)/shard_map/ppermute | solution.py:33
  435.9 12.5 %collective-permute-start.71 = (f32[1,8,32]{2,1,0:T(8,128)}, f32[1,8,32]{2,1,0:T(8,128)}, u32[]{:S(2)}, u32[]{:S(2)}) collective-permute-start(f32[1,8,32]{2,1,0:T(8,128)} %get-tuple-element.120), channel_id=1, source_target_pairs={{0,16},{4,20},{8,24},{12,28},{16,32},{20,36},{24,40},{28,44},{32,4... | collective-permute-start | bytes 3080 | tf_op jit(solution)/shard_map/ppermute | solution.py:33
  445.3 51.9 %collective-permute-start.22 = (bf16[16,1,32,8,64]{4,3,2,0,1:T(8,128)(2,1)}, bf16[16,1,32,8,64]{4,3,2,0,1:T(8,128)(2,1)}, u32[]{:S(2)}, u32[]{:S(2)}) collective-permute-start(bf16[16,1,32,8,64]{4,3,2,0,1:T(8,128)(2,1)} %get-tuple-element.75), channel_id=1, source_target_pairs={{0,12},{4,0},{8,4},{12,8},{16,28},{20,16},{24,20},{28,24},{32,44},... | collective-permute-start | bytes 1572872 | tf_op jit(solution)/shard_map/ppermute | solution.py:33
  449.8 14.6 %collective-permute-start.65 = (f32[1,8,32]{2,1,0:T(8,128)}, f32[1,8,32]{2,1,0:T(8,128)}, u32[]{:S(2)}, u32[]{:S(2)}) collective-permute-start(f32[1,8,32]{2,1,0:T(8,128)} %get-tuple-element.42), channel_id=1, source_target_pairs={{0,240},{4,244},{8,248},{12,252},{16,0},{20,4},{24,8},{28,12},{32,... | collective-permute-start | bytes 3080 | tf_op jit(solution)/shard_map/ppermute | solution.py:33
  454.4 12.0 %collective-permute-start.72 = (f32[1,8,32]{2,1,0:T(8,128)}, f32[1,8,32]{2,1,0:T(8,128)}, u32[]{:S(2)}, u32[]{:S(2)}) collective-permute-start(f32[1,8,32]{2,1,0:T(8,128)} %get-tuple-element.118), channel_id=1, source_target_pairs={{0,16},{4,20},{8,24},{12,28},{16,32},{20,36},{24,40},{28,44},{32,4... | collective-permute-start | bytes 3080 | tf_op jit(solution)/shard_map/ppermute | solution.py:33
  464.4 17.9 %collective-permute-start.48 = (f32[1,8,32]{2,1,0:T(8,128)}, f32[1,8,32]{2,1,0:T(8,128)}, u32[]{:S(2)}, u32[]{:S(2)}) collective-permute-start(f32[1,8,32]{2,1,0:T(8,128)} %get-tuple-element.135), channel_id=1, source_target_pairs={{0,16},{4,20},{8,24},{12,28},{16,32},{20,36},{24,40},{28,44},{32,4... | collective-permute-start | bytes 3080 | tf_op jit(solution)/shard_map/ppermute | solution.py:33
  467.7 16.9 %collective-permute-start.66 = (f32[1,8,32]{2,1,0:T(8,128)}, f32[1,8,32]{2,1,0:T(8,128)}, u32[]{:S(2)}, u32[]{:S(2)}) collective-permute-start(f32[1,8,32]{2,1,0:T(8,128)} %get-tuple-element.40), channel_id=1, source_target_pairs={{0,240},{4,244},{8,248},{12,252},{16,0},{20,4},{24,8},{28,12},{32,... | collective-permute-start | bytes 3080 | tf_op jit(solution)/shard_map/ppermute | solution.py:33
  477.1 11.9 %collective-permute-start.73 = (f32[1,8,32]{2,1,0:T(8,128)}, f32[1,8,32]{2,1,0:T(8,128)S(1)}, u32[]{:S(2)}, u32[]{:S(2)}) collective-permute-start(f32[1,8,32]{2,1,0:T(8,128)} %get-tuple-element.116), channel_id=1, source_target_pairs={{0,16},{4,20},{8,24},{12,28},{16,32},{20,36},{24,40},{28,44},{32,4... | collective-permute-start | bytes 3080 | tf_op jit(solution)/shard_map/ppermute | solution.py:33
  482.4 30.6 %collective-permute-start.25 = (bf16[16,1,32,8,64]{4,3,2,0,1:T(8,128)(2,1)S(1)}, bf16[16,1,32,8,64]{4,3,2,0,1:T(8,128)(2,1)}, u32[]{:S(2)}, u32[]{:S(2)}) collective-permute-start(bf16[16,1,32,8,64]{4,3,2,0,1:T(8,128)(2,1)S(1)} %get-tuple-element.76), channel_id=1, source_target_pairs={{0,4},{4,8},{8,12},{12,0},{16,20},{20,24},{24,28},{28,16},{32,36},... | collective-permute-start | bytes 1572872 | tf_op jit(solution)/shard_map/ppermute | solution.py:33
  484.7 17.1 %collective-permute-start.75 = (bf16[16,1,8,32,64]{4,3,2,0,1:T(8,128)(2,1)}, bf16[16,1,8,32,64]{4,3,2,0,1:T(8,128)(2,1)S(1)}, u32[]{:S(2)}, u32[]{:S(2)}) collective-permute-start(bf16[16,1,8,32,64]{4,3,2,0,1:T(8,128)(2,1)} %fusion.18), channel_id=1, source_target_pairs={{0,12},{4,0},{8,4},{12,8},{16,28},{20,16},{24,20},{28,24},{32,44},... | collective-permute-start | bytes 1572872 | tf_op jit(solution)/shard_map/ppermute | solution.py:33
  499.8 15.9 %collective-permute-start.23 = (bf16[16,1,32,8,64]{4,3,2,0,1:T(8,128)(2,1)S(1)}, bf16[16,1,32,8,64]{4,3,2,0,1:T(8,128)(2,1)S(1)}, u32[]{:S(2)}, u32[]{:S(2)}) collective-permute-start(bf16[16,1,32,8,64]{4,3,2,0,1:T(8,128)(2,1)S(1)} %fusion.23), channel_id=1, source_target_pairs={{0,12},{4,0},{8,4},{12,8},{16,28},{20,16},{24,20},{28,24},{32,44},... | collective-permute-start | bytes 1572872 | tf_op jit(solution)/shard_map/ppermute | solution.py:33
  506.1 27.5 %collective-permute-start.85 = (bf16[1,8,32,64]{3,2,1,0:T(8,128)(2,1)S(1)}, bf16[1,8,32,64]{3,2,1,0:T(8,128)(2,1)S(1)}, u32[]{:S(2)}, u32[]{:S(2)}) collective-permute-start(bf16[1,8,32,64]{3,2,1,0:T(8,128)(2,1)S(1)} %fusion.112), channel_id=1, source_target_pairs={{0,16},{4,20},{8,24},{12,28},{16,32},{20,36},{24,40},{28,44},{32,4... | collective-permute-start | bytes 98312 | tf_op jit(solution)/shard_map/ppermute | solution.py:33
  508.5 18.3 %collective-permute-start.77 = (bf16[1,8,32,64]{3,2,1,0:T(8,128)(2,1)S(1)}, bf16[1,8,32,64]{3,2,1,0:T(8,128)(2,1)S(1)}, u32[]{:S(2)}, u32[]{:S(2)}) collective-permute-start(bf16[1,8,32,64]{3,2,1,0:T(8,128)(2,1)S(1)} %fusion.111), channel_id=1, source_target_pairs={{0,240},{4,244},{8,248},{12,252},{16,0},{20,4},{24,8},{28,12},{32,... | collective-permute-start | bytes 98312 | tf_op jit(solution)/shard_map/ppermute | solution.py:33
  520.1 11.4 %collective-permute-start.34 = (bf16[1,32,8,64]{3,2,1,0:T(8,128)(2,1)S(1)}, bf16[1,32,8,64]{3,2,1,0:T(8,128)(2,1)S(1)}, u32[]{:S(2)}, u32[]{:S(2)}) collective-permute-start(bf16[1,32,8,64]{3,2,1,0:T(8,128)(2,1)S(1)} %get-tuple-element.101), channel_id=1, source_target_pairs={{0,240},{4,244},{8,248},{12,252},{16,0},{20,4},{24,8},{28,12},{32,... | collective-permute-start | bytes 98312 | tf_op jit(solution)/shard_map/ppermute | solution.py:33
  524.8 15.8 %collective-permute-start.49 = (bf16[1,32,8,64]{3,2,1,0:T(8,128)(2,1)S(1)}, bf16[1,32,8,64]{3,2,1,0:T(8,128)(2,1)S(1)}, u32[]{:S(2)}, u32[]{:S(2)}) collective-permute-start(bf16[1,32,8,64]{3,2,1,0:T(8,128)(2,1)S(1)} %get-tuple-element.102), channel_id=1, source_target_pairs={{0,16},{4,20},{8,24},{12,28},{16,32},{20,36},{24,40},{28,44},{32,4... | collective-permute-start | bytes 98312 | tf_op jit(solution)/shard_map/ppermute | solution.py:33
  534.6 12.9 %collective-permute-start.79 = (bf16[1,8,32,64]{3,2,1,0:T(8,128)(2,1)S(1)}, bf16[1,8,32,64]{3,2,1,0:T(8,128)(2,1)S(1)}, u32[]{:S(2)}, u32[]{:S(2)}) collective-permute-start(bf16[1,8,32,64]{3,2,1,0:T(8,128)(2,1)S(1)} %get-tuple-element.87), channel_id=1, source_target_pairs={{0,240},{4,244},{8,248},{12,252},{16,0},{20,4},{24,8},{28,12},{32,... | collective-permute-start | bytes 98312 | tf_op jit(solution)/shard_map/ppermute | solution.py:33
  541.0 13.9 %collective-permute-start.36 = (bf16[1,32,8,64]{3,2,1,0:T(8,128)(2,1)S(1)}, bf16[1,32,8,64]{3,2,1,0:T(8,128)(2,1)S(1)}, u32[]{:S(2)}, u32[]{:S(2)}) collective-permute-start(bf16[1,32,8,64]{3,2,1,0:T(8,128)(2,1)S(1)} %get-tuple-element.99), channel_id=1, source_target_pairs={{0,240},{4,244},{8,248},{12,252},{16,0},{20,4},{24,8},{28,12},{32,... | collective-permute-start | bytes 98312 | tf_op jit(solution)/shard_map/ppermute | solution.py:33
  548.4 13.3 %collective-permute-start.80 = (bf16[1,8,32,64]{3,2,1,0:T(8,128)(2,1)S(1)}, bf16[1,8,32,64]{3,2,1,0:T(8,128)(2,1)S(1)}, u32[]{:S(2)}, u32[]{:S(2)}) collective-permute-start(bf16[1,8,32,64]{3,2,1,0:T(8,128)(2,1)S(1)} %get-tuple-element.85), channel_id=1, source_target_pairs={{0,240},{4,244},{8,248},{12,252},{16,0},{20,4},{24,8},{28,12},{32,... | collective-permute-start | bytes 98312 | tf_op jit(solution)/shard_map/ppermute | solution.py:33
  555.2 14.0 %collective-permute-start.37 = (bf16[1,32,8,64]{3,2,1,0:T(8,128)(2,1)S(1)}, bf16[1,32,8,64]{3,2,1,0:T(8,128)(2,1)S(1)}, u32[]{:S(2)}, u32[]{:S(2)}) collective-permute-start(bf16[1,32,8,64]{3,2,1,0:T(8,128)(2,1)S(1)} %get-tuple-element.97), channel_id=1, source_target_pairs={{0,240},{4,244},{8,248},{12,252},{16,0},{20,4},{24,8},{28,12},{32,... | collective-permute-start | bytes 98312 | tf_op jit(solution)/shard_map/ppermute | solution.py:33
  562.7 13.5 %collective-permute-start.81 = (bf16[1,8,32,64]{3,2,1,0:T(8,128)(2,1)S(1)}, bf16[1,8,32,64]{3,2,1,0:T(8,128)(2,1)S(1)}, u32[]{:S(2)}, u32[]{:S(2)}) collective-permute-start(bf16[1,8,32,64]{3,2,1,0:T(8,128)(2,1)S(1)} %get-tuple-element.83), channel_id=1, source_target_pairs={{0,240},{4,244},{8,248},{12,252},{16,0},{20,4},{24,8},{28,12},{32,... | collective-permute-start | bytes 98312 | tf_op jit(solution)/shard_map/ppermute | solution.py:33
  569.5 14.2 %collective-permute-start.38 = (bf16[1,32,8,64]{3,2,1,0:T(8,128)(2,1)S(1)}, bf16[1,32,8,64]{3,2,1,0:T(8,128)(2,1)S(1)}, u32[]{:S(2)}, u32[]{:S(2)}) collective-permute-start(bf16[1,32,8,64]{3,2,1,0:T(8,128)(2,1)S(1)} %get-tuple-element.95), channel_id=1, source_target_pairs={{0,240},{4,244},{8,248},{12,252},{16,0},{20,4},{24,8},{28,12},{32,... | collective-permute-start | bytes 98312 | tf_op jit(solution)/shard_map/ppermute | solution.py:33
  574.0 9.6 %collective-permute-start.52 = (bf16[1,32,8,64]{3,2,1,0:T(8,128)(2,1)S(1)}, bf16[1,32,8,64]{3,2,1,0:T(8,128)(2,1)S(1)}, u32[]{:S(2)}, u32[]{:S(2)}) collective-permute-start(bf16[1,32,8,64]{3,2,1,0:T(8,128)(2,1)S(1)} %get-tuple-element.96), channel_id=1, source_target_pairs={{0,16},{4,20},{8,24},{12,28},{16,32},{20,36},{24,40},{28,44},{32,4... | collective-permute-start | bytes 98312 | tf_op jit(solution)/shard_map/ppermute | solution.py:33
  577.2 13.3 %collective-permute-start.82 = (bf16[1,8,32,64]{3,2,1,0:T(8,128)(2,1)S(1)}, bf16[1,8,32,64]{3,2,1,0:T(8,128)(2,1)S(1)}, u32[]{:S(2)}, u32[]{:S(2)}) collective-permute-start(bf16[1,8,32,64]{3,2,1,0:T(8,128)(2,1)S(1)} %get-tuple-element.81), channel_id=1, source_target_pairs={{0,240},{4,244},{8,248},{12,252},{16,0},{20,4},{24,8},{28,12},{32,... | collective-permute-start | bytes 98312 | tf_op jit(solution)/shard_map/ppermute | solution.py:33
  583.9 14.0 %collective-permute-start.39 = (bf16[1,32,8,64]{3,2,1,0:T(8,128)(2,1)S(1)}, bf16[1,32,8,64]{3,2,1,0:T(8,128)(2,1)S(1)}, u32[]{:S(2)}, u32[]{:S(2)}) collective-permute-start(bf16[1,32,8,64]{3,2,1,0:T(8,128)(2,1)S(1)} %get-tuple-element.93), channel_id=1, source_target_pairs={{0,240},{4,244},{8,248},{12,252},{16,0},{20,4},{24,8},{28,12},{32,... | collective-permute-start | bytes 98312 | tf_op jit(solution)/shard_map/ppermute | solution.py:33
  591.4 13.3 %collective-permute-start.83 = (bf16[1,8,32,64]{3,2,1,0:T(8,128)(2,1)S(1)}, bf16[1,8,32,64]{3,2,1,0:T(8,128)(2,1)S(1)}, u32[]{:S(2)}, u32[]{:S(2)}) collective-permute-start(bf16[1,8,32,64]{3,2,1,0:T(8,128)(2,1)S(1)} %get-tuple-element.79), channel_id=1, source_target_pairs={{0,240},{4,244},{8,248},{12,252},{16,0},{20,4},{24,8},{28,12},{32,... | collective-permute-start | bytes 98312 | tf_op jit(solution)/shard_map/ppermute | solution.py:33
  598.2 13.3 %collective-permute-start.40 = (bf16[1,32,8,64]{3,2,1,0:T(8,128)(2,1)S(1)}, bf16[1,32,8,64]{3,2,1,0:T(8,128)(2,1)S(1)}, u32[]{:S(2)}, u32[]{:S(2)}) collective-permute-start(bf16[1,32,8,64]{3,2,1,0:T(8,128)(2,1)S(1)} %get-tuple-element.91), channel_id=1, source_target_pairs={{0,240},{4,244},{8,248},{12,252},{16,0},{20,4},{24,8},{28,12},{32,... | collective-permute-start | bytes 98312 | tf_op jit(solution)/shard_map/ppermute | solution.py:33
  604.9 13.3 %collective-permute-start.84 = (bf16[1,8,32,64]{3,2,1,0:T(8,128)(2,1)S(1)}, bf16[1,8,32,64]{3,2,1,0:T(8,128)(2,1)S(1)}, u32[]{:S(2)}, u32[]{:S(2)}) collective-permute-start(bf16[1,8,32,64]{3,2,1,0:T(8,128)(2,1)S(1)} %get-tuple-element.77), channel_id=1, source_target_pairs={{0,240},{4,244},{8,248},{12,252},{16,0},{20,4},{24,8},{28,12},{32,... | collective-permute-start | bytes 98312 | tf_op jit(solution)/shard_map/ppermute | solution.py:33
  611.7 57.9 %collective-permute-start.41 = (bf16[1,32,8,64]{3,2,1,0:T(8,128)(2,1)S(1)}, bf16[1,32,8,64]{3,2,1,0:T(8,128)(2,1)S(1)}, u32[]{:S(2)}, u32[]{:S(2)}) collective-permute-start(bf16[1,32,8,64]{3,2,1,0:T(8,128)(2,1)S(1)} %get-tuple-element.89), channel_id=1, source_target_pairs={{0,240},{4,244},{8,248},{12,252},{16,0},{20,4},{24,8},{28,12},{32,... | collective-permute-start | bytes 98312 | tf_op jit(solution)/shard_map/ppermute | solution.py:33
  616.3 53.3 %collective-permute-start.55 = (bf16[1,32,8,64]{3,2,1,0:T(8,128)(2,1)S(1)}, bf16[1,32,8,64]{3,2,1,0:T(8,128)(2,1)S(1)}, u32[]{:S(2)}, u32[]{:S(2)}) collective-permute-start(bf16[1,32,8,64]{3,2,1,0:T(8,128)(2,1)S(1)} %get-tuple-element.90), channel_id=1, source_target_pairs={{0,16},{4,20},{8,24},{12,28},{16,32},{20,36},{24,40},{28,44},{32,4... | collective-permute-start | bytes 98312 | tf_op jit(solution)/shard_map/ppermute | solution.py:33
  (144 other events, 4949.2 us)
Sparse Core Ops, SparseCore 0:
  65.6 132.2 all-gather.1
